TPU v7x, 128 devices: a whole 4x4x4 slice. The times are simulated.
128 devices in a mesh: seq: 16 (over x_lo, z, core), batch: 8 (over y, x_hi).
Axes of the slice: x: 4 (x_hi: 2, x_lo: 2; x = x_hi * 2 + x_lo), y: 4, z: 4, core: 2. Of those that a mesh axis runs over, the one named last changes fastest.
Arguments:
- activations: bfloat16 [2, 8192, 1536], P(None, ('seq', 'batch')), may hold values from -6 to 6
- conv_gain: float32 [1536], replicated, may hold values from 0.25 to 1.75
- conv_weight: bfloat16 [5, 1536, 1536], P(None, 'batch'), may hold values from -0.0625 to 0.0625
- attention_gain: float32 [1536], replicated, may hold values from 0.25 to 1.75
- query_weight: bfloat16 [1536, 1536], P('batch'), may hold values from -3 to 3
- key_weight: bfloat16 [1536, 1536], P('batch'), may hold values from -3 to 3
- value_weight: bfloat16 [1536, 1536], P('batch'), may hold values from -0.15625 to 0.15625
- output_weight: bfloat16 [1536, 1536], P('batch'), may hold values from -0.15625 to 0.15625
Outputs:
- block_out: bfloat16 [2, 8192, 1536], P(None, ('seq', 'batch'))
All inputs are finite; a program needn't handle non-finite values.
Results may differ from a plain program's by a relative error of at most 0.015.
Values may be sent and summed in bfloat16 or wider, within the bound.
No kernel may reach another device: no remote copies, remote signals or barrier semaphores. Data moves between devices by JAX's collectives and lax.ppermute only.
A program may use at most 128 MiB of HBM per device.

v0:
```python
import math
import jax
import jax.numpy as jnp
from jax import lax
from jax.sharding import PartitionSpec as P

HD = 192


def with_halo(cells, sides, width):
    for axis, dim in sides:
        count = lax.axis_size(axis)
        ends = count - 1
        head = lax.slice_in_dim(cells, 0, width, axis=dim)
        tail = lax.slice_in_dim(cells, cells.shape[dim] - width, cells.shape[dim], axis=dim)
        cells = jnp.concatenate(
            [
                lax.ppermute(tail, axis, [(i, (i + 1) % count) for i in range(ends)]),
                cells,
                lax.ppermute(head, axis, [((i + 1) % count, i) for i in range(ends)]),
            ],
            axis=dim,
        )
    return cells


def gather_batch(block, axis):
    count = lax.axis_size("batch")
    copies = jnp.broadcast_to(block[None], (count,) + block.shape)
    arrived = jnp.moveaxis(lax.all_to_all(copies, "batch", 0, 0, tiled=False), 0, axis)
    return arrived.reshape(
        block.shape[:axis] + (count * block.shape[axis],) + block.shape[axis + 1 :]
    )


def normalize(rows_in, gain):
    values = rows_in.astype(jnp.float32)
    scale = lax.rsqrt(jnp.mean(values * values, axis=-1, keepdims=True) + 1e-06)
    return values * scale * gain


def shards(
    activations,
    conv_gain,
    conv_weight,
    attention_gain,
    query_weight,
    key_weight,
    value_weight,
    output_weight,
):
    sample_count, own_rows, full_width = activations.shape
    tap_count, local_out, _ = conv_weight.shape
    flank_rows = tap_count // 2
    gathered_in = gather_batch(activations, 1)
    seq_rows = gathered_in.shape[1]
    active = jax.nn.gelu(normalize(gathered_in, conv_gain)).astype(jnp.bfloat16)
    framed = with_halo(active, (("seq", 1),), flank_rows)
    conv_sum = jnp.zeros((sample_count, local_out, seq_rows), jnp.float32)
    for offset in range(tap_count):
        conv_sum = conv_sum + jnp.einsum(
            "std,ed->set",
            framed[:, offset : offset + seq_rows],
            conv_weight[offset],
            preferred_element_type=jnp.float32,
        )
    column_start = lax.axis_index("batch") * local_out
    own_columns = lax.dynamic_slice_in_dim(gathered_in, column_start, local_out, 2)
    residual = jnp.transpose(own_columns, (0, 2, 1)).astype(jnp.float32)
    hidden_part = (residual + conv_sum).astype(jnp.bfloat16)
    hidden_full = gather_batch(hidden_part, 1)
    hidden_float = hidden_full.astype(jnp.float32)
    norm_scale = lax.rsqrt(jnp.mean(hidden_float * hidden_float, axis=1, keepdims=True) + 1e-06)
    normed = (hidden_float * norm_scale * attention_gain[None, :, None]).astype(jnp.bfloat16)
    queries = (
        jnp.einsum("sdt,ed->set", normed, query_weight, preferred_element_type=jnp.float32)
        * HD ** (-0.5)
    ).astype(jnp.bfloat16)
    key_rows = jnp.einsum(
        "sdt,ed->set", normed, key_weight, preferred_element_type=jnp.float32
    ).astype(jnp.bfloat16)
    value_rows = jnp.einsum(
        "sdt,ed->set", normed, value_weight, preferred_element_type=jnp.float32
    ).astype(jnp.bfloat16)
    heads_here = query_weight.shape[0] // HD
    query_heads = queries.reshape(sample_count, heads_here, HD, seq_rows)
    start_max = jnp.full((sample_count, heads_here, seq_rows), -jnp.inf, jnp.float32)
    start_sum = jnp.zeros((sample_count, heads_here, seq_rows), jnp.float32)
    start_acc = jnp.zeros((sample_count, heads_here, HD, seq_rows), jnp.float32)
    key_tile = lax.all_gather(key_rows, "seq", axis=2, tiled=True)
    value_tile = lax.all_gather(value_rows, "seq", axis=2, tiled=True)
    key_count = key_tile.shape[2]
    block_rows = math.gcd(key_count, 512)

    def consume(block_index, running):
        running_max, weight_sum, summed = running
        begin = block_index * block_rows
        key_block = lax.dynamic_slice_in_dim(key_tile, begin, block_rows, 2).reshape(
            sample_count, heads_here, HD, block_rows
        )
        value_block = lax.dynamic_slice_in_dim(value_tile, begin, block_rows, 2).reshape(
            sample_count, heads_here, HD, block_rows
        )
        scores = jnp.einsum(
            "shdq,shdk->shqk", query_heads, key_block, preferred_element_type=jnp.float32
        )
        new_max = jnp.maximum(running_max, jnp.max(scores, axis=-1))
        weights = jnp.exp(scores - new_max[..., None])
        rescale = jnp.exp(running_max - new_max)
        weight_sum = weight_sum * rescale + jnp.sum(weights, axis=-1)
        summed = summed * rescale[:, :, None, :] + jnp.einsum(
            "shqk,shdk->shdq",
            weights.astype(jnp.bfloat16),
            value_block,
            preferred_element_type=jnp.float32,
        )
        return (new_max, weight_sum, summed)

    final_max, weight_sum, summed = lax.fori_loop(
        0, key_count // block_rows, consume, (start_max, start_sum, start_acc)
    )
    attended = (
        (summed / weight_sum[:, :, None, :])
        .astype(jnp.bfloat16)
        .reshape(sample_count, heads_here * HD, seq_rows)
    )
    row_start = lax.axis_index("batch") * own_rows
    own_hidden = jnp.transpose(
        lax.dynamic_slice_in_dim(hidden_full, row_start, own_rows, 2), (0, 2, 1)
    ).astype(jnp.float32)
    batch_count = lax.axis_size("batch")
    partial_rows = jnp.einsum(
        "set,ef->tsf", attended, output_weight, preferred_element_type=jnp.float32
    ).astype(jnp.bfloat16)
    partial_rows = partial_rows.reshape(batch_count, own_rows, sample_count, full_width)
    share_rows = jnp.sum(
        lax.all_to_all(partial_rows, "batch", 0, 0, tiled=False).astype(jnp.float32), axis=0
    )
    branch_rows = jnp.transpose(share_rows, (1, 0, 2))
    result = own_hidden + branch_rows
    return result.astype(jnp.bfloat16)


def solution(mesh):
    placed = (
        P(None, ("seq", "batch"), None),
        P(),
        P(None, "batch", None),
        P(),
        P("batch", None),
        P("batch", None),
        P("batch", None),
        P("batch", None),
    )
    return jax.shard_map(
        shards,
        mesh=mesh,
        in_specs=placed,
        out_specs=P(None, ("seq", "batch"), None),
        check_vma=False,
    )
```

profile of v0, /device:TPU:0, one launch (start us, length us, event | category | flops | bytes accessed | tf_op | source)
XLA Modules:
  0.0 335.0 jit_solution(1888584935394674766)
XLA Ops:
  6.5 3.0 broadcast_in_dim.14
  9.6 7.0 %all-to-all-start = ((bf16[8,2,64,1536]{3,2,1,0:T(8,128)(2,1)}), bf16[8,2,64,1536]{3,2,1,0:T(8,128)(2,1)}, u32[]{:S(2)}, u32[]{:S(2)}) async-start(bf16[8,2,64,1536]{3,2,1,0:T(8,128)(2,1)} %broadcast_in_dim.14), calls=%async_computation | async-start | bytes 6291456 | tf_op jit(solution)/shard_map/all_to_all | solution.py:30
  16.6 39.8 %all-to-all-done = bf16[8,2,64,1536]{3,2,1,0:T(8,128)(2,1)} async-done(((bf16[8,2,64,1536]{3,2,1,0:T(8,128)(2,1)}), bf16[8,2,64,1536]{3,2,1,0:T(8,128)(2,1)}, u32[]{:S(2)}, u32[]{:S(2)}) %all-to-all-start) | async-done | bytes 3145760 | tf_op jit(solution)/shard_map/all_to_all | solution.py:30
  56.4 2.6 fusion.13
  59.1 2.2 copy.63
  61.3 3.0 fusion.29
  64.3 1.3 collective-permute-start.1
  65.6 4.2 %fusion.17 = bf16[2,8,64,1536]{3,2,1,0:T(8,128)(2,1)S(1)} fusion(f32[1536]{0:T(1024)S(1)} %copy-done.5, f32[2,8,64]{2,1,0:T(8,128)S(1)} %add_rsqrt_fusion, bf16[8,2,64,1536]{3,2,1,0:T(8,128)(2,1)} %all-to-all-done), kind=kLoop, calls=%fused_computation.29 | loop fusion | flops 18874368 | bytes 6301696 | tf_op jit(solution)/shard_map/convert_element_type | solution.py:57
  69.8 2.2 fusion.73
  72.5 3.3 collective-permute-start
  75.9 3.2 fusion.32
  79.1 1.2 fusion.37
  80.3 1.2 fusion.39
  81.4 1.3 fusion.63
  83.1 43.2 %all_to_all.15 = bf16[8,2,192,512]{3,2,1,0:T(8,128)(2,1)S(1)} all-to-all(bf16[8,2,192,512]{3,2,1,0:T(8,128)(2,1)S(1)} %broadcast_in_dim.15), channel_id=1, replica_groups=mesh['seq'=16,'batch'=8] {'batch'}, dimensions={0} | all-to-all | bytes 6291456 | tf_op jit(solution)/shard_map/all_to_all | solution.py:30
  126.3 0.7 multiply_reduce_fusion
  127.6 0.8 multiply_convert_fusion
  128.4 0.9 copy-done.1
  129.3 1.6 copy-done.4
  130.9 1.5 fusion.60
  132.5 3.5 %fusion.61 = bf16[2,192,512]{2,1,0:T(8,128)(2,1)} fusion(bf16[2,1536,512]{2,1,0:T(8,128)(2,1)} %copy-done.4, bf16[192,1536]{1,0:T(8,128)(2,1)S(1)} %copy-done.9), kind=kOutput, calls=%fused_computation.72 | convolution fusion | flops 604176384 | bytes 4128768 | tf_op jit(solution)/shard_map/sdt,ed->set/dot_general | solution.py:82
  136.1 2.7 fusion.62
  138.7 34.8 %all-gather.3.cloned.1.call-done = bf16[2,192,8192]{2,1,0:T(8,128)(2,1)} async-done(((bf16[2,192,512]{2,1,0:T(8,128)(2,1)}), bf16[2,192,8192]{2,1,0:T(8,128)(2,1)}) %all-gather.3.cloned.1.call-update) | async-done | bytes 6291472 | tf_op jit(solution)/shard_map/all_gather | solution.py:90
  173.6 45.0 %all-gather.5.cloned.1.call-done = bf16[2,192,8192]{2,1,0:T(8,128)(2,1)} async-done(((bf16[2,192,512]{2,1,0:T(8,128)(2,1)}), bf16[2,192,8192]{2,1,0:T(8,128)(2,1)}) %all-gather.5.cloned.1.call-update) | async-done | bytes 6291472 | tf_op jit(solution)/shard_map/all_gather | solution.py:91
  218.5 56.6 %while.18 = (s32[]{:T(128)}, f32[2,1,512]{2,0,1:T(2,128)S(1)}, f32[2,1,512]{2,0,1:T(2,128)S(1)}, f32[2,1,192,512]{3,2,0,1:T(8,128)S(1)}, bf16[2,192,8192]{2,1,0:...) while((s32[]{:T(128)}, f32[2,1,512]{2,0,1:T(2,128)S(1)}, ...), condition=%wide.region_5.0_spmd.clone, body=%wide.region_2.0_spmd.clone.sunk | while | flops 405870592 | bytes 9109687 | solution.py:119
  218.5 1.5 bitcast_reduce_fusion.2
  220.4 1.6 fusion.101
  222.1 1.5 bitcast_reduce_fusion.2
  223.9 1.6 fusion.101
  225.6 1.5 bitcast_reduce_fusion.2
  227.4 1.6 fusion.101
  229.1 1.5 bitcast_reduce_fusion.2
  231.0 1.6 fusion.101
  232.7 1.5 bitcast_reduce_fusion.2
  234.5 1.6 fusion.101
  236.2 1.5 bitcast_reduce_fusion.2
  238.0 1.6 fusion.101
  239.7 1.5 bitcast_reduce_fusion.2
  241.6 1.6 fusion.101
  243.3 1.5 bitcast_reduce_fusion.2
  245.1 1.6 fusion.101
  246.8 1.5 bitcast_reduce_fusion.2
  248.7 1.6 fusion.101
  250.4 1.5 bitcast_reduce_fusion.2
  252.2 1.6 fusion.101
  253.9 1.5 bitcast_reduce_fusion.2
  255.7 1.6 fusion.101
  257.4 1.5 bitcast_reduce_fusion.2
  259.3 1.6 fusion.101
  261.0 1.5 bitcast_reduce_fusion.2
  262.8 1.6 fusion.101
  264.5 1.5 bitcast_reduce_fusion.2
  266.3 1.6 fusion.101
  268.0 1.5 bitcast_reduce_fusion.2
  269.9 1.6 fusion.101
  271.6 1.5 bitcast_reduce_fusion.2
  273.4 1.6 fusion.101
  275.1 1.0 convolution_convert_fusion
  276.1 2.0 copy.67
  278.1 6.6 %all-to-all-start.2 = ((bf16[8,64,2,1536]{3,1,2,0:T(8,128)(2,1)}), bf16[8,64,2,1536]{3,1,2,0:T(8,128)(2,1)}, u32[]{:S(2)}, u32[]{:S(2)}) async-start(bf16[8,64,2,1536]{3,1,2,0:T(8,128)(2,1)} %copy.67), calls=%async_computation.2 | async-start | bytes 6291456 | tf_op jit(solution)/shard_map/all_to_all | solution.py:137
  284.7 1.4 constant_dynamic-slice_fusion
  286.4 38.6 %all-to-all-done.2 = bf16[8,64,2,1536]{3,1,2,0:T(8,128)(2,1)} async-done(((bf16[8,64,2,1536]{3,1,2,0:T(8,128)(2,1)}), bf16[8,64,2,1536]{3,1,2,0:T(8,128)(2,1)}, u32[]{:S(2)}, u32[]{:S(2)}) %all-to-all-start.2) | async-done | bytes 3145760 | tf_op jit(solution)/shard_map/all_to_all | solution.py:137
  324.9 2.4 convert_reduce_fusion
  327.3 0.8 fusion.66
  (102 shorter events, 7.3 us)
Async XLA Ops:
  6.5 268.6 %copy-start = (bf16[192,1536]{1,0:T(8,128)(2,1)S(1)}, bf16[192,1536]{1,0:T(8,128)(2,1)}, u32[]{:S(2)}) copy-start(bf16[192,1536]{1,0:T(8,128)(2,1)} %param.17) | copy-start | bytes 1769476
  9.6 46.8 %all-to-all-start = ((bf16[8,2,64,1536]{3,2,1,0:T(8,128)(2,1)}), bf16[8,2,64,1536]{3,2,1,0:T(8,128)(2,1)}, u32[]{:S(2)}, u32[]{:S(2)}) async-start(bf16[8,2,64,1536]{3,2,1,0:T(8,128)(2,1)} %broadcast_in_dim.14), calls=%async_computation | async-start | bytes 6291456 | tf_op jit(solution)/shard_map/all_to_all | solution.py:30
  16.6 157.0 %all-gather.3.cloned.1.call-start = ((), (), s32[]{:S(2)}) async-start(), calls=%async_computation.3 | async-start | bytes 6684672 | tf_op jit(solution)/shard_map/all_gather | solution.py:90
  59.1 2.2 copy-start.5
  64.3 5.6 %copy-start.2 = (bf16[2,512,1536]{2,1,0:T(8,128)(2,1)}, bf16[2,512,1536]{2,1,0:T(8,128)(2,1)S(1)}, u32[]{:S(2)}) copy-start(bf16[2,512,1536]{2,1,0:T(8,128)(2,1)S(1)} %fusion.29) | copy-start | bytes 9437188
  64.3 11.5 %collective-permute-start.1 = (bf16[2,2,1536]{2,1,0:T(2,128)(2,1)S(1)}, bf16[2,2,1536]{2,1,0:T(2,128)(2,1)S(1)}, u32[]{:S(2)}, u32[]{:S(2)}) collective-permute-start(bf16[2,2,1536]{2,1,0:T(2,128)(2,1)S(1)} %get-tuple-element.175), channel_id=1, source_target_pairs={{8,0},{16,8},{24,16},{32,24},{40,32},{48,40},{56,48},{64,56},{72,6... | collective-permute-start | bytes 36872 | tf_op jit(solution)/shard_map/ppermute | solution.py:20
  72.5 6.5 %copy-start.3 = (bf16[2,512,1536]{2,1,0:T(8,128)(2,1)S(1)}, bf16[2,512,1536]{2,1,0:T(8,128)(2,1)}, u32[]{:S(2)}) copy-start(bf16[2,512,1536]{2,1,0:T(8,128)(2,1)} %copy-done.2) | copy-start | bytes 9437188
  72.5 6.5 %copy-start.7 = (bf16[5,192,1536]{2,1,0:T(8,128)(2,1)S(1)}, bf16[5,192,1536]{2,1,0:T(8,128)(2,1)}, u32[]{:S(2)}) copy-start(bf16[5,192,1536]{2,1,0:T(8,128)(2,1)} %param.12) | copy-start | bytes 8847364
  72.5 7.7 %collective-permute-start = (bf16[2,2,1536]{2,1,0:T(2,128)(2,1)S(1)}, bf16[2,2,1536]{2,1,0:T(2,128)(2,1)S(1)}, u32[]{:S(2)}, u32[]{:S(2)}) collective-permute-start(bf16[2,2,1536]{2,1,0:T(2,128)(2,1)S(1)} %get-tuple-element.174), channel_id=1, source_target_pairs={{0,8},{8,16},{16,24},{24,32},{32,40},{40,48},{48,56},{56,64},{64,7... | collective-permute-start | bytes 36872 | tf_op jit(solution)/shard_map/ppermute | solution.py:18
  126.9 0.7 copy-start.6
  127.6 1.6 copy-start.1
  127.6 3.3 copy-start.8
  129.3 1.6 copy-start.4
  130.9 1.6 copy-start.9
  132.5 3.6 %copy-start.10 = (bf16[192,1536]{1,0:T(8,128)(2,1)S(1)}, bf16[192,1536]{1,0:T(8,128)(2,1)}, u32[]{:S(2)}) copy-start(bf16[192,1536]{1,0:T(8,128)(2,1)} %param.14) | copy-start | bytes 1769476
  132.5 86.0 %all-gather.5.cloned.1.call-start = ((), (), s32[]{:S(2)}) async-start(), calls=%async_computation.4 | async-start | bytes 6684672 | tf_op jit(solution)/shard_map/all_gather | solution.py:91
  278.1 46.8 %all-to-all-start.2 = ((bf16[8,64,2,1536]{3,1,2,0:T(8,128)(2,1)}), bf16[8,64,2,1536]{3,1,2,0:T(8,128)(2,1)}, u32[]{:S(2)}, u32[]{:S(2)}) async-start(bf16[8,64,2,1536]{3,1,2,0:T(8,128)(2,1)} %copy.67), calls=%async_computation.2 | async-start | bytes 6291456 | tf_op jit(solution)/shard_map/all_to_all | solution.py:137
Sparse Core Ops, SparseCore 0:
  132.6 40.9 all-gather.2
  175.2 43.2 all-gather.4
where the time goes:
time: 337 us; the launch traced here: 335 us
  waiting for transfers between devices  158 us (47%)
  matrix products  68.1 us (20%)
  blocking collectives  43.2 us (13%)
  other arithmetic  19.8 us (6%)
  starting transfers between devices  18.3 us (5%)
  between operations  13.7 us (4%)
  local copies, waits for them, and re-layouts  12.9 us (4%)
    all_gather x1, waiting for transfers between devices, shards(): value_tile = lax.all_gather(value_rows, 'seq', axis=2, tiled=True)  45 us
    all_to_all x1, blocking collectives, gather_batch(): lax.all_to_all(copies, 'batch', 0, 0, tiled=False)  43.2 us
    all_to_all x1, waiting for transfers between devices, gather_batch(): lax.all_to_all(copies, 'batch', 0, 0, tiled=False)  39.8 us
    all_to_all x1, waiting for transfers between devices, shards(): lax.all_to_all(partial_rows, 'batch', 0, 0, tiled=False).astype(jnp.float32)  38.6 us
    all_gather x1, waiting for transfers between devices, shards(): key_tile = lax.all_gather(key_rows, 'seq', axis=2, tiled=True)  34.8 us
    dot_general x16, matrix products, consume(): jnp.einsum('shqk,shdk->shdq', weights.astype(jnp.bfloat16), value_block,...  26.3 us
    dot_general x16, matrix products, consume(): jnp.einsum('shdq,shdk->shqk', query_heads, key_block, preferred_element_t...  24 us
    dot_general x5, matrix products, shards(): jnp.einsum('std,ed->set', framed[:, offset:offset + seq_rows], conv_weigh...  9.08 us
  transfers between devices with their start and end apart: 6, of which 4 were waited for; matrix products, arithmetic and copies ran while one was open for 6% of the time, Pallas kernels for 0%

commit v1 on v0

--- a/solution.py
+++ b/solution.py
@@ -87,7 +87,9 @@
     start_max = jnp.full((sample_count, heads_here, seq_rows), -jnp.inf, jnp.float32)
     start_sum = jnp.zeros((sample_count, heads_here, seq_rows), jnp.float32)
     start_acc = jnp.zeros((sample_count, heads_here, HD, seq_rows), jnp.float32)
-    key_tile = lax.all_gather(key_rows, "seq", axis=2, tiled=True)
+    key_tile = jnp.concatenate(
+        lax.all_to_all(jnp.stack([key_rows] * lax.axis_size("seq")), "seq", 0, 0), axis=2
+    )
     value_tile = lax.all_gather(value_rows, "seq", axis=2, tiled=True)
     key_count = key_tile.shape[2]
     block_rows = math.gcd(key_count, 512)

time: 337 us -> 378 us (1.12)
  waiting for transfers between devices: 158 us -> 181 us
  local copies, waits for them, and re-layouts: 12.9 us -> 23.2 us
  starting transfers between devices: 18.3 us -> 24.6 us
    all_to_all x0 -> x1, waiting for transfers between devices: none -> 103 us  [shards(): lax.all_to_all(jnp.stack([key_rows] * lax.axis_size('seq')), 'seq', 0, 0)]
    all_gather x1, waiting for transfers between devices: 45 us -> 0.01 us  [shards(): value_tile = lax.all_gather(value_rows, 'seq', axis=2, tiled=True)]
    all_gather x1 -> x0, waiting for transfers between devices: 34.8 us -> none  [shards(): key_tile = lax.all_gather(key_rows, 'seq', axis=2, tiled=True)]
    all_to_all x0 -> x1, starting transfers between devices: none -> 8.54 us  [shards(): lax.all_to_all(jnp.stack([key_rows] * lax.axis_size('seq')), 'seq', 0, 0)]
    reshape x0 -> x1, local copies, waits for them, and re-layouts: none -> 6.34 us  [shards(): jnp.concatenate(lax.all_to_all(jnp.stack([key_rows] * lax.axis_size('seq'...]
  transfers between devices with their start and end apart: 6 -> 6, of which waited for: 4 -> 3; matrix products, arithmetic and copies ran while one was open for 6% -> 8% of each run, Pallas kernels for 0% -> 0%
where the time goes in v1:
time: 378 us; the launch traced here: 376 us
  waiting for transfers between devices  181 us (48%)
  matrix products  70.2 us (19%)
  blocking collectives  42.5 us (11%)
  starting transfers between devices  24.6 us (7%)
  local copies, waits for them, and re-layouts  23.2 us (6%)
  other arithmetic  19.8 us (5%)
  between operations  13.7 us (4%)
    all_to_all x1, waiting for transfers between devices, shards(): lax.all_to_all(jnp.stack([key_rows] * lax.axis_size('seq')), 'seq', 0, 0)  103 us
    all_to_all x1, blocking collectives, gather_batch(): lax.all_to_all(copies, 'batch', 0, 0, tiled=False)  42.5 us
    all_to_all x1, waiting for transfers between devices, gather_batch(): lax.all_to_all(copies, 'batch', 0, 0, tiled=False)  39.8 us
    all_to_all x1, waiting for transfers between devices, shards(): lax.all_to_all(partial_rows, 'batch', 0, 0, tiled=False).astype(jnp.float32)  38.2 us
    dot_general x16, matrix products, consume(): jnp.einsum('shqk,shdk->shdq', weights.astype(jnp.bfloat16), value_block,...  26.3 us
    dot_general x16, matrix products, consume(): jnp.einsum('shdq,shdk->shqk', query_heads, key_block, preferred_element_t...  26 us
    dot_general x5, matrix products, shards(): jnp.einsum('std,ed->set', framed[:, offset:offset + seq_rows], conv_weigh...  9.23 us
    all_to_all x1, starting transfers between devices, shards(): lax.all_to_all(jnp.stack([key_rows] * lax.axis_size('seq')), 'seq', 0, 0)  8.54 us
  transfers between devices with their start and end apart: 6, of which 3 were waited for; matrix products, arithmetic and copies ran while one was open for 8% of the time, Pallas kernels for 0%

profile of v1, /device:TPU:0, one launch (start us, length us, event | category | flops | bytes accessed | tf_op | source)
XLA Modules:
  0.0 376.3 jit_solution(10111257264327265974)
XLA Ops:
  6.5 3.0 broadcast_in_dim.14
  9.6 7.0 %all-to-all-start = ((bf16[8,2,64,1536]{3,2,1,0:T(8,128)(2,1)}), bf16[8,2,64,1536]{3,2,1,0:T(8,128)(2,1)}, u32[]{:S(2)}, u32[]{:S(2)}) async-start(bf16[8,2,64,1536]{3,2,1,0:T(8,128)(2,1)} %broadcast_in_dim.14), calls=%async_computation | async-start | bytes 6291456 | tf_op jit(solution)/shard_map/all_to_all | solution.py:30
  16.6 39.8 %all-to-all-done = bf16[8,2,64,1536]{3,2,1,0:T(8,128)(2,1)} async-done(((bf16[8,2,64,1536]{3,2,1,0:T(8,128)(2,1)}), bf16[8,2,64,1536]{3,2,1,0:T(8,128)(2,1)}, u32[]{:S(2)}, u32[]{:S(2)}) %all-to-all-start) | async-done | bytes 3145760 | tf_op jit(solution)/shard_map/all_to_all | solution.py:30
  56.4 2.6 fusion.13
  59.1 2.2 copy.65
  61.3 3.0 fusion.29
  64.3 1.3 collective-permute-start
  65.6 1.3 collective-permute-start.1
  66.9 4.2 %fusion.17 = bf16[2,8,64,1536]{3,2,1,0:T(8,128)(2,1)S(1)} fusion(f32[1536]{0:T(1024)S(1)} %copy-done.5, f32[2,8,64]{2,1,0:T(8,128)S(1)} %add_rsqrt_fusion, bf16[8,2,64,1536]{3,2,1,0:T(8,128)(2,1)} %all-to-all-done), kind=kLoop, calls=%fused_computation.29 | loop fusion | flops 18874368 | bytes 6301696 | tf_op jit(solution)/shard_map/convert_element_type | solution.py:57
  71.1 2.2 fusion.73
  73.8 3.4 fusion.32
  77.7 1.2 fusion.37
  78.9 1.2 fusion.39
  80.1 1.3 fusion.63
  81.7 42.5 %all_to_all.20 = bf16[8,2,192,512]{3,2,1,0:T(8,128)(2,1)S(1)} all-to-all(bf16[8,2,192,512]{3,2,1,0:T(8,128)(2,1)S(1)} %broadcast_in_dim.15), channel_id=1, replica_groups=mesh['seq'=16,'batch'=8] {'batch'}, dimensions={0} | all-to-all | bytes 6291456 | tf_op jit(solution)/shard_map/all_to_all | solution.py:30
  126.4 0.9 copy-done.1
  127.3 1.6 copy-done.4
  128.9 1.5 fusion.61
  130.5 2.7 fusion.60
  133.2 3.4 stack.2
  136.5 8.5 %all-to-all-start.2 = ((bf16[16,2,192,512]{3,2,1,0:T(8,128)(2,1)}), bf16[16,2,192,512]{3,2,1,0:T(8,128)(2,1)}, u32[]{:S(2)}, u32[]{:S(2)}) async-start(bf16[16,2,192,512]{3,2,1,0:T(8,128)(2,1)} %stack.2), calls=%async_computation.2 | async-start | bytes 12582912 | tf_op jit(solution)/shard_map/all_to_all | solution.py:91
  145.1 3.5 fusion.62
  148.6 103.4 %all-to-all-done.2 = bf16[16,2,192,512]{3,2,1,0:T(8,128)(2,1)} async-done(((bf16[16,2,192,512]{3,2,1,0:T(8,128)(2,1)}), bf16[16,2,192,512]{3,2,1,0:T(8,128)(2,1)}, u32[]{:S(2)}, u32[]{:S(2)}) %all-to-all-start.2) | async-done | bytes 6291488 | tf_op jit(solution)/shard_map/all_to_all | solution.py:91
  252.0 6.3 %copy.76 = bf16[16,2,24,8,512]{4,3,0,2,1:T(8,128)(2,1)} copy(bf16[16,2,24,8,512]{4,3,2,1,0:T(8,128)(2,1)} %bitcast.42) | data formatting | bytes 12582912 | tf_op jit(solution)/shard_map/reshape | solution.py:90
  258.4 58.6 %while.18 = (s32[]{:T(128)}, f32[2,1,512]{2,0,1:T(2,128)S(1)}, f32[2,1,512]{2,0,1:T(2,128)S(1)}, f32[2,1,192,512]{3,2,0,1:T(8,128)S(1)}, bf16[2,192,8192]{2,1,0:...) while((s32[]{:T(128)}, f32[2,1,512]{2,0,1:T(2,128)S(1)}, ...), condition=%wide.region_5.0_spmd.clone, body=%wide.region_2.0_spmd.clone.sunk | while | flops 405870592 | bytes 9109679 | solution.py:121
  258.4 1.6 bitcast_reduce_fusion.2
  260.0 1.6 fusion.101
  262.0 1.6 bitcast_reduce_fusion.2
  263.7 1.6 fusion.101
  265.7 1.6 bitcast_reduce_fusion.2
  267.3 1.6 fusion.101
  269.3 1.6 bitcast_reduce_fusion.2
  271.0 1.6 fusion.101
  273.0 1.6 bitcast_reduce_fusion.2
  274.7 1.6 fusion.101
  276.7 1.6 bitcast_reduce_fusion.2
  278.3 1.6 fusion.101
  280.3 1.6 bitcast_reduce_fusion.2
  282.0 1.6 fusion.101
  284.0 1.6 bitcast_reduce_fusion.2
  285.6 1.6 fusion.101
  287.6 1.6 bitcast_reduce_fusion.2
  289.3 1.6 fusion.101
  291.3 1.6 bitcast_reduce_fusion.2
  293.0 1.6 fusion.101
  295.0 1.6 bitcast_reduce_fusion.2
  296.6 1.6 fusion.101
  298.6 1.6 bitcast_reduce_fusion.2
  300.3 1.6 fusion.101
  302.3 1.6 bitcast_reduce_fusion.2
  303.9 1.6 fusion.101
  305.9 1.6 bitcast_reduce_fusion.2
  307.6 1.6 fusion.101
  309.6 1.6 bitcast_reduce_fusion.2
  311.3 1.6 fusion.101
  313.3 1.6 bitcast_reduce_fusion.2
  314.9 1.6 fusion.101
  316.9 1.0 convolution_convert_fusion
  318.0 2.0 copy.70
  319.9 6.4 %all-to-all-start.3 = ((bf16[8,64,2,1536]{3,1,2,0:T(8,128)(2,1)}), bf16[8,64,2,1536]{3,1,2,0:T(8,128)(2,1)}, u32[]{:S(2)}, u32[]{:S(2)}) async-start(bf16[8,64,2,1536]{3,1,2,0:T(8,128)(2,1)} %copy.70), calls=%async_computation.3 | async-start | bytes 6291456 | tf_op jit(solution)/shard_map/all_to_all | solution.py:139
  326.3 1.4 constant_dynamic-slice_fusion
  328.0 38.2 %all-to-all-done.3 = bf16[8,64,2,1536]{3,1,2,0:T(8,128)(2,1)} async-done(((bf16[8,64,2,1536]{3,1,2,0:T(8,128)(2,1)}), bf16[8,64,2,1536]{3,1,2,0:T(8,128)(2,1)}, u32[]{:S(2)}, u32[]{:S(2)}) %all-to-all-start.3) | async-done | bytes 3145760 | tf_op jit(solution)/shard_map/all_to_all | solution.py:139
  366.2 2.4 convert_reduce_fusion
  368.6 0.8 fusion.66
  (103 shorter events, 9.2 us)
Async XLA Ops:
  6.5 310.4 %copy-start = (bf16[192,1536]{1,0:T(8,128)(2,1)S(1)}, bf16[192,1536]{1,0:T(8,128)(2,1)}, u32[]{:S(2)}) copy-start(bf16[192,1536]{1,0:T(8,128)(2,1)} %param.17) | copy-start | bytes 1769476
  9.6 46.8 %all-to-all-start = ((bf16[8,2,64,1536]{3,2,1,0:T(8,128)(2,1)}), bf16[8,2,64,1536]{3,2,1,0:T(8,128)(2,1)}, u32[]{:S(2)}, u32[]{:S(2)}) async-start(bf16[8,2,64,1536]{3,2,1,0:T(8,128)(2,1)} %broadcast_in_dim.14), calls=%async_computation | async-start | bytes 6291456 | tf_op jit(solution)/shard_map/all_to_all | solution.py:30
  16.6 241.8 %all-gather.2.cloned.1.call-start = ((), (), s32[]{:S(2)}) async-start(), calls=%async_computation.4 | async-start | bytes 6684672 | tf_op jit(solution)/shard_map/all_gather | solution.py:93
  59.1 2.2 copy-start.5
  64.3 6.8 %copy-start.2 = (bf16[2,512,1536]{2,1,0:T(8,128)(2,1)}, bf16[2,512,1536]{2,1,0:T(8,128)(2,1)S(1)}, u32[]{:S(2)}) copy-start(bf16[2,512,1536]{2,1,0:T(8,128)(2,1)S(1)} %fusion.29) | copy-start | bytes 9437188
  64.3 14.6 %collective-permute-start = (bf16[2,2,1536]{2,1,0:T(2,128)(2,1)S(1)}, bf16[2,2,1536]{2,1,0:T(2,128)(2,1)S(1)}, u32[]{:S(2)}, u32[]{:S(2)}) collective-permute-start(bf16[2,2,1536]{2,1,0:T(2,128)(2,1)S(1)} %get-tuple-element.174), channel_id=1, source_target_pairs={{0,8},{8,16},{16,24},{24,32},{32,40},{40,48},{48,56},{56,64},{64,7... | collective-permute-start | bytes 36872 | tf_op jit(solution)/shard_map/ppermute | solution.py:18
  65.6 8.2 %collective-permute-start.1 = (bf16[2,2,1536]{2,1,0:T(2,128)(2,1)S(1)}, bf16[2,2,1536]{2,1,0:T(2,128)(2,1)S(1)}, u32[]{:S(2)}, u32[]{:S(2)}) collective-permute-start(bf16[2,2,1536]{2,1,0:T(2,128)(2,1)S(1)} %get-tuple-element.175), channel_id=1, source_target_pairs={{8,0},{16,8},{24,16},{32,24},{40,32},{48,40},{56,48},{64,56},{72,6... | collective-permute-start | bytes 36872 | tf_op jit(solution)/shard_map/ppermute | solution.py:20
  73.8 3.4 copy-start.3
  73.8 3.9 %copy-start.7 = (bf16[5,192,1536]{2,1,0:T(8,128)(2,1)S(1)}, bf16[5,192,1536]{2,1,0:T(8,128)(2,1)}, u32[]{:S(2)}) copy-start(bf16[5,192,1536]{2,1,0:T(8,128)(2,1)} %param.12) | copy-start | bytes 8847364
  124.9 0.7 copy-start.6
  125.6 1.7 copy-start.1
  125.6 3.3 copy-start.8
  127.3 1.7 copy-start.4
  128.9 1.6 copy-start.9
  136.5 8.6 %copy-start.10 = (bf16[192,1536]{1,0:T(8,128)(2,1)S(1)}, bf16[192,1536]{1,0:T(8,128)(2,1)}, u32[]{:S(2)}) copy-start(bf16[192,1536]{1,0:T(8,128)(2,1)} %param.14) | copy-start | bytes 1769476
  136.5 115.5 %all-to-all-start.2 = ((bf16[16,2,192,512]{3,2,1,0:T(8,128)(2,1)}), bf16[16,2,192,512]{3,2,1,0:T(8,128)(2,1)}, u32[]{:S(2)}, u32[]{:S(2)}) async-start(bf16[16,2,192,512]{3,2,1,0:T(8,128)(2,1)} %stack.2), calls=%async_computation.2 | async-start | bytes 12582912 | tf_op jit(solution)/shard_map/all_to_all | solution.py:91
  319.9 46.3 %all-to-all-start.3 = ((bf16[8,64,2,1536]{3,1,2,0:T(8,128)(2,1)}), bf16[8,64,2,1536]{3,1,2,0:T(8,128)(2,1)}, u32[]{:S(2)}, u32[]{:S(2)}) async-start(bf16[8,64,2,1536]{3,1,2,0:T(8,128)(2,1)} %copy.70), calls=%async_computation.3 | async-start | bytes 6291456 | tf_op jit(solution)/shard_map/all_to_all | solution.py:139
Sparse Core Ops, SparseCore 0:
  130.6 110.7 all-gather.1
